TPU v7x, 512 devices: a whole 4x8x8 slice. The times are simulated.
512 devices in a mesh: sub: 128 (over z_hi, x, y, core), scen: 4 (over z_lo).
Axes of the slice: x: 4, y: 8, z: 8 (z_hi: 2, z_lo: 4; z = z_hi * 4 + z_lo), core: 2. Of those that a mesh axis runs over, the one named last changes fastest.
Arguments:
- inverse_matrix: bfloat16 [128, 1024, 1024], P('sub'), may hold values from -1 to 1
- objective_grad: bfloat16 [48, 128, 64, 1024], P(None, 'sub', 'scen'), may hold values from -6 to 6
- final_adjoint: float32 [128, 64, 1024], P('sub', 'scen'), may hold values from -6 to 6
- companion: float32 [128, 1024], P('sub'), may hold values from 0.95 to 0.995
- port_node: int32 [128, 4, 8], P('sub'), may hold values from 0 to 1023
- line_count: int32 [128, 4], P('sub'), may hold values from 1 to 8, as said below
- line_delay: int32 [128, 4, 8], P('sub'), may hold values from 24 to 47, as said below
- line_admittance: float32 [128, 4, 8], P('sub'), may hold values from 0.3 to 1.2
- later_history: float32 [128, 4, 8, 48, 64], P('sub', None, None, None, 'scen'), may hold values from -6 to 6
- conv_node: int32 [128, 16], P('sub'), may hold values from 0 to 1023
- conv_drive: float32 [128, 48, 64, 16], P('sub', None, 'scen'), may hold values from -0.25 to 0.25
- fault_bus: int32 [64], P('scen'), may hold values from 0 to 131071
- fault_current: float32 [48, 64], P(None, 'scen'), may hold values from -12 to 12
- fault_voltage: float32 [48, 64], P(None, 'scen'), may hold values from -2 to 2
Outputs:
- adjoint_start: float32 [128, 64, 1024], P('sub', 'scen')
- earlier_history: float32 [128, 4, 8, 48, 64], P('sub', None, None, None, 'scen')
- control_sens: float32 [128, 16], P('sub')
- fault_sens: float32 [64], P('scen')
Inputs may be any that keep to these rules, and one draw needn't show every extreme that they name: line_count[p, e] equals line_count of the partner subnetwork in the opposite direction; the most is reached in every draw. `line_delay`: both ends of a line have the same delay; both ends of the range are reached in every draw.
All inputs are finite; a program needn't handle non-finite values.
Results may differ from a plain program's by a relative error of at most 0.0088.
Values sent between devices are 32-bit elements; how exact they have to be, the bound alone decides.
No kernel may reach another device: no remote copies, remote signals or barrier semaphores. Data moves between devices by JAX's collectives and lax.ppermute only.
A program may use at most 64 MiB of HBM per device.

v0:
```python
import jax
import jax.numpy as jnp
import numpy as np
from jax.sharding import Mesh
from jax import lax
from jax.sharding import PartitionSpec as P

PRECISE = lax.Precision.HIGHEST
SUB = ("z_hi", "x", "y", "core")
SUB_SIZES = (2, 4, 8, 2)


def sum_over_sub(value):
    for axis in reversed(SUB):
        value = lax.psum(value, axis)
    return value


def passed_along(value, axis, steps):
    count = lax.axis_size(axis)
    pairs = [(source, (source + steps) % count) for source in range(count)]
    return lax.ppermute(value, axis, pairs)


def body(
    inverse_matrix,
    objective_grad,
    final_adjoint,
    companion,
    port_node,
    line_count,
    line_delay,
    line_admittance,
    later_history,
    conv_node,
    conv_drive,
    fault_bus,
    fault_current,
    fault_voltage,
):
    node_count = inverse_matrix.shape[1]
    scen_rows = objective_grad.shape[2]
    slot_count = port_node.shape[2]
    port_total = 4 * slot_count
    conv_count = conv_node.shape[1]
    block_len = later_history.shape[3] // 2
    blocks = objective_grad.shape[0] // block_len
    sub_count = lax.axis_size(SUB)
    grid_width = max(2, sub_count // 16)
    offsets = (1, -1, grid_width, -grid_width)
    opposite = (1, 0, 3, 2)
    sub_index = lax.axis_index(SUB)
    weights = inverse_matrix[0]
    live_mask = (lax.iota(jnp.int32, slot_count)[None, :] < line_count[0][:, None]).astype(
        jnp.float32
    )
    node_iota = lax.iota(jnp.int32, node_count)
    pick_table = jnp.concatenate(
        [
            node_iota[:, None] == port_node[0].reshape(port_total)[None, :],
            node_iota[:, None] == conv_node[0][None, :],
        ],
        axis=1,
    ).astype(jnp.float32)
    spread_table = jnp.transpose(pick_table[:, :port_total])
    line_scale = (line_admittance[0] * live_mask).reshape(port_total)
    fault_table = (node_iota[None, :] == (fault_bus - sub_index * node_count)[:, None]).astype(
        jnp.float32
    )
    window = later_history[0]
    adjoint_next = final_adjoint[0]
    control_local = jnp.zeros((conv_count,), jnp.float32)
    fault_local = jnp.zeros((scen_rows,), jnp.float32)
    block_rows = lax.iota(jnp.int32, block_len)
    time_iota = lax.iota(jnp.int32, 2 * block_len)

    def one_step(adjoint_prev, inputs):
        grad_now, inflow_now, current_now = inputs
        right_side = (
            grad_now.astype(jnp.float32)
            + companion[0][None, :] * adjoint_prev
            + inflow_now
            + current_now[:, None] * fault_table
        )
        adjoint = jnp.dot(
            right_side.astype(jnp.bfloat16), weights, preferred_element_type=jnp.float32
        )
        return (adjoint, adjoint)

    for block_id in reversed(range(blocks)):
        block_start = block_id * block_len
        target = block_rows[None, None, :] + line_delay[0][:, :, None] - block_len
        time_table = (target[..., None] == time_iota).astype(jnp.float32)
        picked = (
            jnp.einsum("ecji,ecis->jsec", time_table, window, precision=PRECISE).reshape(
                block_len * scen_rows, port_total
            )
            * line_scale[None, :]
        )
        inflow = jnp.dot(picked, spread_table, precision=PRECISE).reshape(
            block_len, scen_rows, node_count
        )
        adjoint_next, adjoint_block = lax.scan(
            one_step,
            adjoint_next,
            (
                objective_grad[block_start : block_start + block_len, 0],
                inflow,
                fault_current[block_start : block_start + block_len],
            ),
            reverse=True,
        )
        samples = jnp.dot(
            adjoint_block.reshape(block_len * scen_rows, node_count), pick_table, precision=PRECISE
        )
        series = (
            jnp.transpose(
                samples[:, :port_total].reshape(block_len, scen_rows, 4, slot_count), (2, 3, 0, 1)
            )
            * live_mask[:, :, None, None]
        )
        outbound = series.reshape(4, slot_count, block_len * scen_rows)
        control_term = jnp.sum(
            samples[:, port_total:].reshape(block_len, scen_rows, conv_count)
            * conv_drive[0, block_start : block_start + block_len],
            axis=(0, 1),
        )
        fault_term = jnp.sum(
            jnp.sum(adjoint_block * fault_table[None], axis=2)
            * fault_voltage[block_start : block_start + block_len],
            axis=0,
        )
        control_local = control_local + lax.psum(control_term, "scen")
        fault_local = fault_local + fault_term
        received = jnp.stack(
            [
                passed_along(outbound[opposite[direction]], SUB, -offsets[direction])
                for direction in range(4)
            ]
        )
        window = jnp.concatenate(
            [received.reshape(4, slot_count, block_len, scen_rows), window[:, :, :block_len]],
            axis=2,
        )
    fault_local = sum_over_sub(fault_local)
    return (adjoint_next[None], window[None], control_local[None], fault_local)


def solution(mesh):
    sub_mesh = Mesh(
        np.asarray(mesh.devices).reshape(SUB_SIZES + (mesh.shape["scen"],)), SUB + ("scen",)
    )
    return jax.shard_map(
        body,
        mesh=sub_mesh,
        in_specs=(
            P(SUB, None, None),
            P(None, SUB, "scen", None),
            P(SUB, "scen", None),
            P(SUB, None),
            P(SUB, None, None),
            P(SUB, None),
            P(SUB, None, None),
            P(SUB, None, None),
            P(SUB, None, None, None, "scen"),
            P(SUB, None),
            P(SUB, None, "scen", None),
            P("scen"),
            P(None, "scen"),
            P(None, "scen"),
        ),
        out_specs=(P(SUB, "scen", None), P(SUB, None, None, None, "scen"), P(SUB, None), P("scen")),
        check_vma=False,
    )
```

profile of v0, /device:TPU:4, one launch (start us, length us, event | category | flops | bytes accessed | tf_op | source)
XLA Modules:
  0.0 258.3 jit_solution(13217957040212197619)
XLA Ops:
  6.0 2.5 slice_bitcast_fusion
  9.3 2.0 fusion.45
  12.7 45.9 %while.34 = (s32[]{:T(128)}, f32[16,1024]{1,0:T(8,128)S(1)}, f32[24,16,1024]{2,1,0:T(8,128)}, bf16[24,16,1024]{2,1,0:T(8,128)(2,1)}, f32[1,1024]{1,0:T(1,128)S(1...) while((s32[]{:T(128)}, f32[16,1024]{1,0:T(8,128)S(1)}, ...), condition=%wide.region_1.2_spmd.clone, body=%wide.region_0.1_spmd.clone.sunk | while | flops 33685504 | bytes 2528637 | solution.py:103
  12.7 1.9 bitcast_dynamic-update-slice_fusion.4
  20.4 1.9 bitcast_dynamic-update-slice_fusion.4
  24.2 1.9 bitcast_dynamic-update-slice_fusion.4
  29.9 1.9 bitcast_dynamic-update-slice_fusion.4
  41.4 1.9 bitcast_dynamic-update-slice_fusion.4
  45.2 1.9 bitcast_dynamic-update-slice_fusion.4
  51.0 1.9 bitcast_dynamic-update-slice_fusion.4
  52.9 1.9 bitcast_dynamic-update-slice_fusion.4
  54.8 1.9 bitcast_dynamic-update-slice_fusion.4
  56.7 1.9 bitcast_dynamic-update-slice_fusion.4
  58.7 2.3 fusion.57
  63.4 4.8 %collective-permute-start = (f32[8,384]{1,0:T(8,128)}, f32[8,384]{1,0:T(8,128)S(1)}, u32[]{:S(2)}, u32[]{:S(2)}) collective-permute-start(f32[8,384]{1,0:T(8,128)} %squeeze.91), channel_id=1, source_target_pairs={{0,508},{4,0},{8,4},{12,8},{16,12},{20,16},{24,20},{28,24},{32,28}... | collective-permute-start | bytes 36872 | tf_op jit(solution)/shard_map/ppermute | solution.py:22
  68.2 1.9 collective-permute-start.1
  70.8 5.3 %collective-permute-start.2 = (f32[8,384]{1,0:T(8,128)}, f32[8,384]{1,0:T(8,128)}, u32[]{:S(2)}, u32[]{:S(2)}) collective-permute-start(f32[8,384]{1,0:T(8,128)} %squeeze.93), channel_id=1, source_target_pairs={{0,480},{4,484},{8,488},{12,492},{16,496},{20,500},{24,504},{28,50... | collective-permute-start | bytes 36872 | tf_op jit(solution)/shard_map/ppermute | solution.py:22
  76.3 4.4 %collective-permute-start.3 = (f32[8,384]{1,0:T(8,128)S(1)}, f32[8,384]{1,0:T(8,128)}, u32[]{:S(2)}, u32[]{:S(2)}) collective-permute-start(f32[8,384]{1,0:T(8,128)S(1)} %squeeze.94), channel_id=1, source_target_pairs={{0,32},{4,36},{8,40},{12,44},{16,48},{20,52},{24,56},{28,60},{32,6... | collective-permute-start | bytes 36872 | tf_op jit(solution)/shard_map/ppermute | solution.py:22
  90.7 2.0 fusion.43
  94.1 62.0 %while.35 = (s32[]{:T(128)}, f32[16,1024]{1,0:T(8,128)S(1)}, f32[24,16,1024]{2,1,0:T(8,128)}, bf16[24,16,1024]{2,1,0:T(8,128)(2,1)S(1)}, f32[1,1024]{1,0:T(1,128...) while((s32[]{:T(128)}, f32[16,1024]{1,0:T(8,128)S(1)}, ...), condition=%wide.region_3.4_spmd.clone, body=%wide.region_2.3_spmd.clone.sunk | while | flops 33685504 | bytes 2529533 | solution.py:103
  125.8 1.9 bitcast_dynamic-update-slice_fusion.5
  141.3 1.9 bitcast_dynamic-update-slice_fusion.5
  156.1 2.3 multiply_reduce_fusion
  159.9 6.1 %collective-permute-start.4 = (f32[8,384]{1,0:T(8,128)S(1)}, f32[8,384]{1,0:T(8,128)S(1)}, u32[]{:S(2)}, u32[]{:S(2)}) collective-permute-start(f32[8,384]{1,0:T(8,128)S(1)} %squeeze.95), channel_id=1, source_target_pairs={{0,508},{4,0},{8,4},{12,8},{16,12},{20,16},{24,20},{28,24},{32,28}... | collective-permute-start | bytes 36872 | tf_op jit(solution)/shard_map/ppermute | solution.py:22
  166.1 1.9 collective-permute-start.5
  168.1 3.0 %collective-permute-start.6 = (f32[8,384]{1,0:T(8,128)S(1)}, f32[8,384]{1,0:T(8,128)S(1)}, u32[]{:S(2)}, u32[]{:S(2)}) collective-permute-start(f32[8,384]{1,0:T(8,128)S(1)} %squeeze.97), channel_id=1, source_target_pairs={{0,480},{4,484},{8,488},{12,492},{16,496},{20,500},{24,504},{28,50... | collective-permute-start | bytes 36872 | tf_op jit(solution)/shard_map/ppermute | solution.py:22
  171.3 6.7 %collective-permute-start.7 = (f32[8,384]{1,0:T(8,128)S(1)}, f32[8,384]{1,0:T(8,128)S(1)}, u32[]{:S(2)}, u32[]{:S(2)}) collective-permute-start(f32[8,384]{1,0:T(8,128)S(1)} %squeeze.98), channel_id=1, source_target_pairs={{0,32},{4,36},{8,40},{12,44},{16,48},{20,52},{24,56},{28,60},{32,6... | collective-permute-start | bytes 36872 | tf_op jit(solution)/shard_map/ppermute | solution.py:22
  178.9 2.5 psum.44
  181.4 18.4 %psum.45 = f32[16]{0:T(128)S(1)} all-reduce(f32[16]{0:T(128)S(1)} %psum.44), channel_id=1, replica_groups=mesh['z_hi'=2,'x'=4,'y'=8,'core'=2,'scen'=4] {'y'}, use_global_device_ids=true, to_apply=%region_13.14 | all-reduce | flops 16 | bytes 128 | tf_op jit(solution)/shard_map/psum | solution.py:15
  199.8 32.4 %psum.46 = f32[16]{0:T(128)S(1)} all-reduce(f32[16]{0:T(128)S(1)} %psum.45), channel_id=1, replica_groups=mesh['z_hi'=2,'x'=4,'y'=8,'core'=2,'scen'=4] {'x'}, use_global_device_ids=true, to_apply=%region_14.15 | all-reduce | flops 16 | bytes 128 | tf_op jit(solution)/shard_map/psum | solution.py:15
  232.2 12.4 %psum.47 = f32[16]{0:T(128)} all-reduce(f32[16]{0:T(128)S(1)} %psum.46), channel_id=1, replica_groups=mesh['z_hi'=2,'x'=4,'y'=8,'core'=2,'scen'=4] {'z_hi'}, use_global_device_ids=true, to_apply=%region_15.16 | all-reduce | flops 16 | bytes 128 | tf_op jit(solution)/shard_map/psum | solution.py:15
  244.6 12.1 %psum.48 = f32[16]{0:T(128)} all-reduce(f32[16]{0:T(128)S(1)} %add.151), channel_id=1, replica_groups=mesh['z_hi'=2,'x'=4,'y'=8,'core'=2,'scen'=4] {'scen'}, use_global_device_ids=true, to_apply=%region_5.6 | all-reduce | flops 16 | bytes 128 | tf_op jit(solution)/shard_map/psum | solution.py:133
  (265 shorter events, 111.0 us)
Async XLA Ops:
  3.6 5.7 %copy-start.24 = (s32[32]{0:T(128)}, s32[32]{0:T(128)S(1)}, u32[]{:S(2)}) copy-start(s32[32]{0:T(128)S(1)} %eq.71) | copy-start | bytes 388
  6.0 2.5 copy-start.20
  6.0 3.3 %copy-start.29 = (s32[16]{0:T(128)S(1)}, s32[16]{0:T(128)}, u32[]{:S(2)}) copy-start(s32[16]{0:T(128)} %param.29) | copy-start | bytes 196
  9.2 49.5 %copy-start.11 = (pred[1024,32]{0,1:T(8,128)(4,1)}, pred[1024,32]{0,1:T(8,128)(4,1)S(1)}, u32[]{:S(2)}) copy-start(pred[1024,32]{0,1:T(8,128)(4,1)S(1)} %iota_compare_fusion.5) | copy-start | bytes 98308
  9.3 3.4 %copy-start.26 = (f32[32]{0:T(128)}, f32[32]{0:T(128)S(1)}, u32[]{:S(2)}) copy-start(f32[32]{0:T(128)S(1)} %broadcast_select_fusion) | copy-start | bytes 388
  9.3 3.4 %copy-start = (bf16[1,1024,1024]{2,1,0:T(8,128)(2,1)S(1)}, bf16[1,1024,1024]{2,1,0:T(8,128)(2,1)}, u32[]{:S(2)}) copy-start(bf16[1,1024,1024]{2,1,0:T(8,128)(2,1)} %param.18) | copy-start | bytes 6291460
  9.3 3.4 %copy-start.3 = (f32[1,16,1024]{2,1,0:T(8,128)S(1)}, f32[1,16,1024]{2,1,0:T(8,128)}, u32[]{:S(2)}) copy-start(f32[1,16,1024]{2,1,0:T(8,128)} %param.20) | copy-start | bytes 196612
  9.3 3.4 %copy-start.9 = (f32[1,1024]{1,0:T(1,128)S(1)}, f32[1,1024]{1,0:T(1,128)}, u32[]{:S(2)}) copy-start(f32[1,1024]{1,0:T(1,128)} %param.21) | copy-start | bytes 12292
  12.7 45.9 %copy-start.28 = (s32[1,16]{1,0:T(1,128)S(1)}, s32[1,16]{1,0:T(1,128)}, u32[]{:S(2)}) copy-start(s32[1,16]{1,0:T(1,128)} %param.27) | copy-start | bytes 196
  61.6 19.8 %copy-start.8 = (f32[1,48,16,16]{1,3,2,0:T(8,128)S(1)}, f32[1,48,16,16]{1,3,2,0:T(8,128)}, u32[]{:S(2)}) copy-start(f32[1,48,16,16]{1,3,2,0:T(8,128)} %param.28) | copy-start | bytes 147460
  61.6 20.4 %copy-start.21 = (f32[48,16]{0,1:T(8,128)S(1)}, f32[48,16]{0,1:T(8,128)}, u32[]{:S(2)}) copy-start(f32[48,16]{0,1:T(8,128)} %param.31) | copy-start | bytes 9220
  61.8 20.3 %copy-start.22 = (f32[24,16]{0,1:T(8,128)S(1)}, f32[24,16]{0,1:T(8,128)}, u32[]{:S(2)}) copy-start(f32[24,16]{0,1:T(8,128)} %get-tuple-element.466) | copy-start | bytes 4612
  63.4 23.4 %collective-permute-start = (f32[8,384]{1,0:T(8,128)}, f32[8,384]{1,0:T(8,128)S(1)}, u32[]{:S(2)}, u32[]{:S(2)}) collective-permute-start(f32[8,384]{1,0:T(8,128)} %squeeze.91), channel_id=1, source_target_pairs={{0,508},{4,0},{8,4},{12,8},{16,12},{20,16},{24,20},{28,24},{32,28}... | collective-permute-start | bytes 36872 | tf_op jit(solution)/shard_map/ppermute | solution.py:22
  68.2 18.7 %collective-permute-start.1 = (f32[8,384]{1,0:T(8,128)S(1)}, f32[8,384]{1,0:T(8,128)S(1)}, u32[]{:S(2)}, u32[]{:S(2)}) collective-permute-start(f32[8,384]{1,0:T(8,128)S(1)} %squeeze.92), channel_id=1, source_target_pairs={{0,4},{4,8},{8,12},{12,16},{16,20},{20,24},{24,28},{28,32},{32,36}... | collective-permute-start | bytes 36872 | tf_op jit(solution)/shard_map/ppermute | solution.py:22
  70.8 16.3 %collective-permute-start.2 = (f32[8,384]{1,0:T(8,128)}, f32[8,384]{1,0:T(8,128)}, u32[]{:S(2)}, u32[]{:S(2)}) collective-permute-start(f32[8,384]{1,0:T(8,128)} %squeeze.93), channel_id=1, source_target_pairs={{0,480},{4,484},{8,488},{12,492},{16,496},{20,500},{24,504},{28,50... | collective-permute-start | bytes 36872 | tf_op jit(solution)/shard_map/ppermute | solution.py:22
  76.3 11.8 %collective-permute-start.3 = (f32[8,384]{1,0:T(8,128)S(1)}, f32[8,384]{1,0:T(8,128)}, u32[]{:S(2)}, u32[]{:S(2)}) collective-permute-start(f32[8,384]{1,0:T(8,128)S(1)} %squeeze.94), channel_id=1, source_target_pairs={{0,32},{4,36},{8,40},{12,44},{16,48},{20,52},{24,56},{28,60},{32,6... | collective-permute-start | bytes 36872 | tf_op jit(solution)/shard_map/ppermute | solution.py:22
  85.2 5.5 %copy-start.25 = (s32[32]{0:T(128)S(1)}, s32[32]{0:T(128)}, u32[]{:S(2)}) copy-start(s32[32]{0:T(128)} %copy-done.24) | copy-start | bytes 388
  85.2 5.5 %copy-start.27 = (f32[32]{0:T(128)S(1)}, f32[32]{0:T(128)}, u32[]{:S(2)}) copy-start(f32[32]{0:T(128)} %copy-done.26) | copy-start | bytes 388
  88.1 2.5 copy-start.4
  94.1 62.0 %copy-start.13 = (f32[16,1024]{1,0:T(8,128)S(1)}, f32[16,1024]{1,0:T(8,128)}, u32[]{:S(2)}) copy-start(f32[16,1024]{1,0:T(8,128)} %fusion.55) | copy-start | bytes 196612
  156.1 2.4 copy-start.1
  156.1 2.4 copy-start.12
  159.4 18.6 %copy-start.16 = (f32[384,16]{0,1:T(8,128)S(1)}, f32[384,16]{0,1:T(8,128)}, u32[]{:S(2)}) copy-start(f32[384,16]{0,1:T(8,128)} %squeeze.100) | copy-start | bytes 73732
  159.4 18.6 %copy-start.17 = (f32[384,16]{0,1:T(8,128)S(1)}, f32[384,16]{0,1:T(8,128)}, u32[]{:S(2)}) copy-start(f32[384,16]{0,1:T(8,128)} %squeeze.99) | copy-start | bytes 73732
  159.4 19.4 %copy-start.18 = (f32[24,16]{1,0:T(8,128)S(1)}, f32[24,16]{1,0:T(8,128)}, u32[]{:S(2)}) copy-start(f32[24,16]{1,0:T(8,128)} %copy.62) | copy-start | bytes 4612
  159.4 19.4 %copy-start.19 = (f32[24,16]{1,0:T(8,128)S(1)}, f32[24,16]{1,0:T(8,128)}, u32[]{:S(2)}) copy-start(f32[24,16]{1,0:T(8,128)} %copy.63) | copy-start | bytes 4612
  159.6 97.8 %copy-start.5 = (f32[1,8,24,16]{2,3,1,0:T(8,128)S(1)}, f32[1,8,24,16]{2,3,1,0:T(8,128)}, u32[]{:S(2)}) copy-start(f32[1,8,24,16]{2,3,1,0:T(8,128)} %copy-done.4) | copy-start | bytes 36868
  159.6 97.8 %copy-start.7 = (f32[1,8,24,16]{2,3,1,0:T(8,128)S(1)}, f32[1,8,24,16]{2,3,1,0:T(8,128)}, u32[]{:S(2)}) copy-start(f32[1,8,24,16]{2,3,1,0:T(8,128)} %copy-done.6) | copy-start | bytes 36868
  159.9 96.8 %collective-permute-start.4 = (f32[8,384]{1,0:T(8,128)S(1)}, f32[8,384]{1,0:T(8,128)S(1)}, u32[]{:S(2)}, u32[]{:S(2)}) collective-permute-start(f32[8,384]{1,0:T(8,128)S(1)} %squeeze.95), channel_id=1, source_target_pairs={{0,508},{4,0},{8,4},{12,8},{16,12},{20,16},{24,20},{28,24},{32,28}... | collective-permute-start | bytes 36872 | tf_op jit(solution)/shard_map/ppermute | solution.py:22
  166.1 90.8 %collective-permute-start.5 = (f32[8,384]{1,0:T(8,128)S(1)}, f32[8,384]{1,0:T(8,128)S(1)}, u32[]{:S(2)}, u32[]{:S(2)}) collective-permute-start(f32[8,384]{1,0:T(8,128)S(1)} %squeeze.96), channel_id=1, source_target_pairs={{0,4},{4,8},{8,12},{12,16},{16,20},{20,24},{24,28},{28,32},{32,36}... | collective-permute-start | bytes 36872 | tf_op jit(solution)/shard_map/ppermute | solution.py:22
  168.1 88.9 %collective-permute-start.6 = (f32[8,384]{1,0:T(8,128)S(1)}, f32[8,384]{1,0:T(8,128)S(1)}, u32[]{:S(2)}, u32[]{:S(2)}) collective-permute-start(f32[8,384]{1,0:T(8,128)S(1)} %squeeze.97), channel_id=1, source_target_pairs={{0,480},{4,484},{8,488},{12,492},{16,496},{20,500},{24,504},{28,50... | collective-permute-start | bytes 36872 | tf_op jit(solution)/shard_map/ppermute | solution.py:22
  171.3 86.0 %collective-permute-start.7 = (f32[8,384]{1,0:T(8,128)S(1)}, f32[8,384]{1,0:T(8,128)S(1)}, u32[]{:S(2)}, u32[]{:S(2)}) collective-permute-start(f32[8,384]{1,0:T(8,128)S(1)} %squeeze.98), channel_id=1, source_target_pairs={{0,32},{4,36},{8,40},{12,44},{16,48},{20,52},{24,56},{28,60},{32,6... | collective-permute-start | bytes 36872 | tf_op jit(solution)/shard_map/ppermute | solution.py:22
  (6 other events, 10.4 us)
where the time goes:
time: 262 us; the launch traced here: 258 us
  matrix products  101 us (39%)
  blocking collectives  77.8 us (30%)
  local copies, waits for them, and re-layouts  35.8 us (14%)
  starting transfers between devices  34.2 us (13%)
  other arithmetic  7.85 us (3%)
    dot_general x48, matrix products, one_step(): jnp.dot(right_side.astype(jnp.bfloat16), weights, preferred_element_type=...  91 us
    psum x4, blocking collectives, sum_over_sub(): value = lax.psum(value, axis)  65.6 us
    ppermute x8, starting transfers between devices, passed_along(): return lax.ppermute(value, axis, pairs)  34.2 us
    mul x48, local copies, waits for them, and re-layouts, one_step(): current_now[:, None] * fault_table  16.5 us
    psum x1, blocking collectives, body(): control_local = control_local + lax.psum(control_term, 'scen')  12.1 us
  transfers between devices with their start and end apart: 8, of which 0 were waited for; matrix products, arithmetic and copies ran while one was open for 4% of the time, Pallas kernels for 0%

commit v1 on v0

--- a/solution.py
+++ b/solution.py
@@ -12,7 +12,7 @@
 
 def sum_over_sub(value):
     for axis in reversed(SUB):
-        value = lax.psum(value, axis)
+        value = lax.all_gather(value, axis).sum(axis=0)
     return value
 
 

time: 262 us -> 271 us (1.034)
  local copies, waits for them, and re-layouts: 35.8 us -> 42.1 us
    psum x4 -> x0, blocking collectives: 65.6 us -> none  [sum_over_sub(): value = lax.psum(value, axis)]
    unnamed x0 -> x4, blocking collectives: none -> 65.1 us
    unnamed x64 -> x73, local copies, waits for them, and re-layouts: 2.87 us -> 8.84 us
  transfers between devices with their start and end apart: 8 -> 8, of which waited for: 0 -> 0; matrix products, arithmetic and copies ran while one was open for 4% -> 6% of each run, Pallas kernels for 0% -> 0%
where the time goes in v1:
time: 271 us; the launch traced here: 267 us
  matrix products  101 us (37%)
  blocking collectives  77.2 us (28%)
  local copies, waits for them, and re-layouts  42.1 us (16%)
  starting transfers between devices  34.2 us (13%)
  other arithmetic  8.51 us (3%)
  between operations  3.96 us (1%)
    dot_general x48, matrix products, one_step(): jnp.dot(right_side.astype(jnp.bfloat16), weights, preferred_element_type=...  91 us
    unnamed x4, blocking collectives  65.1 us
    ppermute x8, starting transfers between devices, passed_along(): return lax.ppermute(value, axis, pairs)  34.2 us
    mul x48, local copies, waits for them, and re-layouts, one_step(): current_now[:, None] * fault_table  16.5 us
    psum x1, blocking collectives, body(): control_local = control_local + lax.psum(control_term, 'scen')  12.1 us
    unnamed x73, local copies, waits for them, and re-layouts  8.84 us
  transfers between devices with their start and end apart: 8, of which 0 were waited for; matrix products, arithmetic and copies ran while one was open for 6% of the time, Pallas kernels for 0%

profile of v1, /device:TPU:4, one launch (start us, length us, event | category | flops | bytes accessed | tf_op | source)
XLA Modules:
  0.0 267.3 jit_solution(66789912903651155)
XLA Ops:
  6.0 2.4 slice_bitcast_fusion
  9.3 2.0 fusion.45
  12.6 45.9 %while.34 = (s32[]{:T(128)}, f32[16,1024]{1,0:T(8,128)S(1)}, f32[24,16,1024]{2,1,0:T(8,128)}, bf16[24,16,1024]{2,1,0:T(8,128)(2,1)}, f32[1,1024]{1,0:T(1,128)S(1...) while((s32[]{:T(128)}, f32[16,1024]{1,0:T(8,128)S(1)}, ...), condition=%wide.region_1.2_spmd.clone, body=%wide.region_0.1_spmd.clone.sunk | while | flops 33685504 | bytes 2528637 | solution.py:103
  14.6 1.9 bitcast_dynamic-update-slice_fusion.4
  18.4 1.9 bitcast_dynamic-update-slice_fusion.4
  24.1 1.9 bitcast_dynamic-update-slice_fusion.4
  35.6 1.9 bitcast_dynamic-update-slice_fusion.4
  39.4 1.9 bitcast_dynamic-update-slice_fusion.4
  45.2 1.9 bitcast_dynamic-update-slice_fusion.4
  47.1 1.9 bitcast_dynamic-update-slice_fusion.4
  49.0 1.9 bitcast_dynamic-update-slice_fusion.4
  52.8 1.9 bitcast_dynamic-update-slice_fusion.4
  54.7 1.9 bitcast_dynamic-update-slice_fusion.4
  58.7 2.3 fusion.57
  63.3 4.8 %collective-permute-start = (f32[8,384]{1,0:T(8,128)}, f32[8,384]{1,0:T(8,128)S(1)}, u32[]{:S(2)}, u32[]{:S(2)}) collective-permute-start(f32[8,384]{1,0:T(8,128)} %squeeze.91), channel_id=1, source_target_pairs={{0,508},{4,0},{8,4},{12,8},{16,12},{20,16},{24,20},{28,24},{32,28}... | collective-permute-start | bytes 36872 | tf_op jit(solution)/shard_map/ppermute | solution.py:22
  68.2 1.9 collective-permute-start.1
  70.8 5.3 %collective-permute-start.2 = (f32[8,384]{1,0:T(8,128)}, f32[8,384]{1,0:T(8,128)}, u32[]{:S(2)}, u32[]{:S(2)}) collective-permute-start(f32[8,384]{1,0:T(8,128)} %squeeze.93), channel_id=1, source_target_pairs={{0,480},{4,484},{8,488},{12,492},{16,496},{20,500},{24,504},{28,50... | collective-permute-start | bytes 36872 | tf_op jit(solution)/shard_map/ppermute | solution.py:22
  76.2 4.4 %collective-permute-start.3 = (f32[8,384]{1,0:T(8,128)S(1)}, f32[8,384]{1,0:T(8,128)}, u32[]{:S(2)}, u32[]{:S(2)}) collective-permute-start(f32[8,384]{1,0:T(8,128)S(1)} %squeeze.94), channel_id=1, source_target_pairs={{0,32},{4,36},{8,40},{12,44},{16,48},{20,52},{24,56},{28,60},{32,6... | collective-permute-start | bytes 36872 | tf_op jit(solution)/shard_map/ppermute | solution.py:22
  98.6 2.0 fusion.43
  101.9 62.0 %while.35 = (s32[]{:T(128)}, f32[16,1024]{1,0:T(8,128)S(1)}, f32[24,16,1024]{2,1,0:T(8,128)}, bf16[24,16,1024]{2,1,0:T(8,128)(2,1)S(1)}, f32[1,1024]{1,0:T(1,128...) while((s32[]{:T(128)}, f32[16,1024]{1,0:T(8,128)S(1)}, ...), condition=%wide.region_3.4_spmd.clone, body=%wide.region_2.3_spmd.clone.sunk | while | flops 33685504 | bytes 2529533 | solution.py:103
  125.8 1.9 bitcast_dynamic-update-slice_fusion.5
  141.4 1.9 bitcast_dynamic-update-slice_fusion.5
  163.9 2.3 multiply_reduce_fusion
  167.7 6.1 %collective-permute-start.4 = (f32[8,384]{1,0:T(8,128)S(1)}, f32[8,384]{1,0:T(8,128)S(1)}, u32[]{:S(2)}, u32[]{:S(2)}) collective-permute-start(f32[8,384]{1,0:T(8,128)S(1)} %squeeze.95), channel_id=1, source_target_pairs={{0,508},{4,0},{8,4},{12,8},{16,12},{20,16},{24,20},{28,24},{32,28}... | collective-permute-start | bytes 36872 | tf_op jit(solution)/shard_map/ppermute | solution.py:22
  173.9 1.9 collective-permute-start.5
  175.9 3.0 %collective-permute-start.6 = (f32[8,384]{1,0:T(8,128)S(1)}, f32[8,384]{1,0:T(8,128)S(1)}, u32[]{:S(2)}, u32[]{:S(2)}) collective-permute-start(f32[8,384]{1,0:T(8,128)S(1)} %squeeze.97), channel_id=1, source_target_pairs={{0,480},{4,484},{8,488},{12,492},{16,496},{20,500},{24,504},{28,50... | collective-permute-start | bytes 36872 | tf_op jit(solution)/shard_map/ppermute | solution.py:22
  179.0 6.7 %collective-permute-start.7 = (f32[8,384]{1,0:T(8,128)S(1)}, f32[8,384]{1,0:T(8,128)S(1)}, u32[]{:S(2)}, u32[]{:S(2)}) collective-permute-start(f32[8,384]{1,0:T(8,128)S(1)} %squeeze.98), channel_id=1, source_target_pairs={{0,32},{4,36},{8,40},{12,44},{16,48},{20,52},{24,56},{28,60},{32,6... | collective-permute-start | bytes 36872 | tf_op jit(solution)/shard_map/ppermute | solution.py:22
  186.8 2.5 all-reduce
  189.6 18.4 %all-reduce.1 = f32[128]{0:T(128)S(1)} all-reduce(f32[128]{0:T(128)S(1)} %dynamic-update-slice.1), channel_id=3, replica_groups=mesh['z_hi'=2,'x'=4,'y'=8,'core'=2,'scen'=4] {'y'}, use_global_device_ids=true, to_apply=%add.1 | all-reduce | flops 128 | bytes 1024
  208.3 32.4 %all-reduce.2 = f32[64]{0:T(128)S(1)} all-reduce(f32[64]{0:T(128)S(1)} %dynamic-update-slice.2), channel_id=4, replica_groups=mesh['z_hi'=2,'x'=4,'y'=8,'core'=2,'scen'=4] {'x'}, use_global_device_ids=true, to_apply=%add.2 | all-reduce | flops 64 | bytes 512
  241.1 11.9 %all-reduce.3 = f32[32]{0:T(128)S(1)} all-reduce(f32[32]{0:T(128)S(1)} %dynamic-update-slice.3), channel_id=5, replica_groups=mesh['z_hi'=2,'x'=4,'y'=8,'core'=2,'scen'=4] {'z_hi'}, use_global_device_ids=true, to_apply=%add.3 | all-reduce | flops 32 | bytes 256
  253.6 12.1 %psum.16 = f32[16]{0:T(128)} all-reduce(f32[16]{0:T(128)S(1)} %add.153), channel_id=1, replica_groups=mesh['z_hi'=2,'x'=4,'y'=8,'core'=2,'scen'=4] {'scen'}, use_global_device_ids=true, to_apply=%region_5.6 | all-reduce | flops 16 | bytes 128 | tf_op jit(solution)/shard_map/psum | solution.py:133
  (284 shorter events, 118.0 us)
Async XLA Ops:
  3.6 5.7 %copy-start.24 = (s32[32]{0:T(128)}, s32[32]{0:T(128)S(1)}, u32[]{:S(2)}) copy-start(s32[32]{0:T(128)S(1)} %eq.71) | copy-start | bytes 388
  5.9 2.5 copy-start.20
  6.0 3.2 %copy-start.29 = (s32[16]{0:T(128)S(1)}, s32[16]{0:T(128)}, u32[]{:S(2)}) copy-start(s32[16]{0:T(128)} %param.29) | copy-start | bytes 196
  9.2 49.5 %copy-start.11 = (pred[1024,32]{0,1:T(8,128)(4,1)}, pred[1024,32]{0,1:T(8,128)(4,1)S(1)}, u32[]{:S(2)}) copy-start(pred[1024,32]{0,1:T(8,128)(4,1)S(1)} %iota_compare_fusion.5) | copy-start | bytes 98308
  9.2 3.4 %copy-start.26 = (f32[32]{0:T(128)}, f32[32]{0:T(128)S(1)}, u32[]{:S(2)}) copy-start(f32[32]{0:T(128)S(1)} %broadcast_select_fusion) | copy-start | bytes 388
  9.2 3.4 %copy-start = (bf16[1,1024,1024]{2,1,0:T(8,128)(2,1)S(1)}, bf16[1,1024,1024]{2,1,0:T(8,128)(2,1)}, u32[]{:S(2)}) copy-start(bf16[1,1024,1024]{2,1,0:T(8,128)(2,1)} %param.18) | copy-start | bytes 6291460
  9.3 3.4 %copy-start.3 = (f32[1,16,1024]{2,1,0:T(8,128)S(1)}, f32[1,16,1024]{2,1,0:T(8,128)}, u32[]{:S(2)}) copy-start(f32[1,16,1024]{2,1,0:T(8,128)} %param.20) | copy-start | bytes 196612
  9.3 3.3 %copy-start.9 = (f32[1,1024]{1,0:T(1,128)S(1)}, f32[1,1024]{1,0:T(1,128)}, u32[]{:S(2)}) copy-start(f32[1,1024]{1,0:T(1,128)} %param.21) | copy-start | bytes 12292
  12.6 45.9 %copy-start.28 = (s32[1,16]{1,0:T(1,128)S(1)}, s32[1,16]{1,0:T(1,128)}, u32[]{:S(2)}) copy-start(s32[1,16]{1,0:T(1,128)} %param.27) | copy-start | bytes 196
  61.6 19.8 %copy-start.8 = (f32[1,48,16,16]{1,3,2,0:T(8,128)S(1)}, f32[1,48,16,16]{1,3,2,0:T(8,128)}, u32[]{:S(2)}) copy-start(f32[1,48,16,16]{1,3,2,0:T(8,128)} %param.28) | copy-start | bytes 147460
  61.6 20.4 %copy-start.21 = (f32[48,16]{0,1:T(8,128)S(1)}, f32[48,16]{0,1:T(8,128)}, u32[]{:S(2)}) copy-start(f32[48,16]{0,1:T(8,128)} %param.31) | copy-start | bytes 9220
  61.8 20.3 %copy-start.22 = (f32[24,16]{0,1:T(8,128)S(1)}, f32[24,16]{0,1:T(8,128)}, u32[]{:S(2)}) copy-start(f32[24,16]{0,1:T(8,128)} %get-tuple-element.466) | copy-start | bytes 4612
  63.3 31.3 %collective-permute-start = (f32[8,384]{1,0:T(8,128)}, f32[8,384]{1,0:T(8,128)S(1)}, u32[]{:S(2)}, u32[]{:S(2)}) collective-permute-start(f32[8,384]{1,0:T(8,128)} %squeeze.91), channel_id=1, source_target_pairs={{0,508},{4,0},{8,4},{12,8},{16,12},{20,16},{24,20},{28,24},{32,28}... | collective-permute-start | bytes 36872 | tf_op jit(solution)/shard_map/ppermute | solution.py:22
  68.2 26.6 %collective-permute-start.1 = (f32[8,384]{1,0:T(8,128)S(1)}, f32[8,384]{1,0:T(8,128)S(1)}, u32[]{:S(2)}, u32[]{:S(2)}) collective-permute-start(f32[8,384]{1,0:T(8,128)S(1)} %squeeze.92), channel_id=1, source_target_pairs={{0,4},{4,8},{8,12},{12,16},{16,20},{20,24},{24,28},{28,32},{32,36}... | collective-permute-start | bytes 36872 | tf_op jit(solution)/shard_map/ppermute | solution.py:22
  70.8 24.2 %collective-permute-start.2 = (f32[8,384]{1,0:T(8,128)}, f32[8,384]{1,0:T(8,128)}, u32[]{:S(2)}, u32[]{:S(2)}) collective-permute-start(f32[8,384]{1,0:T(8,128)} %squeeze.93), channel_id=1, source_target_pairs={{0,480},{4,484},{8,488},{12,492},{16,496},{20,500},{24,504},{28,50... | collective-permute-start | bytes 36872 | tf_op jit(solution)/shard_map/ppermute | solution.py:22
  76.2 19.7 %collective-permute-start.3 = (f32[8,384]{1,0:T(8,128)S(1)}, f32[8,384]{1,0:T(8,128)}, u32[]{:S(2)}, u32[]{:S(2)}) collective-permute-start(f32[8,384]{1,0:T(8,128)S(1)} %squeeze.94), channel_id=1, source_target_pairs={{0,32},{4,36},{8,40},{12,44},{16,48},{20,52},{24,56},{28,60},{32,6... | collective-permute-start | bytes 36872 | tf_op jit(solution)/shard_map/ppermute | solution.py:22
  93.0 5.5 %copy-start.25 = (s32[32]{0:T(128)S(1)}, s32[32]{0:T(128)}, u32[]{:S(2)}) copy-start(s32[32]{0:T(128)} %copy-done.24) | copy-start | bytes 388
  93.0 5.5 %copy-start.27 = (f32[32]{0:T(128)S(1)}, f32[32]{0:T(128)}, u32[]{:S(2)}) copy-start(f32[32]{0:T(128)} %copy-done.26) | copy-start | bytes 388
  95.9 2.5 copy-start.4
  101.9 62.0 %copy-start.13 = (f32[16,1024]{1,0:T(8,128)S(1)}, f32[16,1024]{1,0:T(8,128)}, u32[]{:S(2)}) copy-start(f32[16,1024]{1,0:T(8,128)} %fusion.55) | copy-start | bytes 196612
  163.9 2.4 copy-start.1
  163.9 2.4 copy-start.12
  167.2 18.6 %copy-start.18 = (f32[24,16]{1,0:T(8,128)S(1)}, f32[24,16]{1,0:T(8,128)}, u32[]{:S(2)}) copy-start(f32[24,16]{1,0:T(8,128)} %copy.62) | copy-start | bytes 4612
  167.2 18.6 %copy-start.19 = (f32[24,16]{1,0:T(8,128)S(1)}, f32[24,16]{1,0:T(8,128)}, u32[]{:S(2)}) copy-start(f32[24,16]{1,0:T(8,128)} %copy.63) | copy-start | bytes 4612
  167.2 18.7 %copy-start.16 = (f32[384,16]{0,1:T(8,128)S(1)}, f32[384,16]{0,1:T(8,128)}, u32[]{:S(2)}) copy-start(f32[384,16]{0,1:T(8,128)} %squeeze.100) | copy-start | bytes 73732
  167.2 18.7 %copy-start.17 = (f32[384,16]{0,1:T(8,128)S(1)}, f32[384,16]{0,1:T(8,128)}, u32[]{:S(2)}) copy-start(f32[384,16]{0,1:T(8,128)} %squeeze.99) | copy-start | bytes 73732
  167.4 99.0 %copy-start.5 = (f32[1,8,24,16]{2,3,1,0:T(8,128)S(1)}, f32[1,8,24,16]{2,3,1,0:T(8,128)}, u32[]{:S(2)}) copy-start(f32[1,8,24,16]{2,3,1,0:T(8,128)} %copy-done.4) | copy-start | bytes 36868
  167.4 99.0 %copy-start.7 = (f32[1,8,24,16]{2,3,1,0:T(8,128)S(1)}, f32[1,8,24,16]{2,3,1,0:T(8,128)}, u32[]{:S(2)}) copy-start(f32[1,8,24,16]{2,3,1,0:T(8,128)} %copy-done.6) | copy-start | bytes 36868
  167.7 98.0 %collective-permute-start.4 = (f32[8,384]{1,0:T(8,128)S(1)}, f32[8,384]{1,0:T(8,128)S(1)}, u32[]{:S(2)}, u32[]{:S(2)}) collective-permute-start(f32[8,384]{1,0:T(8,128)S(1)} %squeeze.95), channel_id=1, source_target_pairs={{0,508},{4,0},{8,4},{12,8},{16,12},{20,16},{24,20},{28,24},{32,28}... | collective-permute-start | bytes 36872 | tf_op jit(solution)/shard_map/ppermute | solution.py:22
  173.9 92.0 %collective-permute-start.5 = (f32[8,384]{1,0:T(8,128)S(1)}, f32[8,384]{1,0:T(8,128)S(1)}, u32[]{:S(2)}, u32[]{:S(2)}) collective-permute-start(f32[8,384]{1,0:T(8,128)S(1)} %squeeze.96), channel_id=1, source_target_pairs={{0,4},{4,8},{8,12},{12,16},{16,20},{20,24},{24,28},{28,32},{32,36}... | collective-permute-start | bytes 36872 | tf_op jit(solution)/shard_map/ppermute | solution.py:22
  175.9 90.2 %collective-permute-start.6 = (f32[8,384]{1,0:T(8,128)S(1)}, f32[8,384]{1,0:T(8,128)S(1)}, u32[]{:S(2)}, u32[]{:S(2)}) collective-permute-start(f32[8,384]{1,0:T(8,128)S(1)} %squeeze.97), channel_id=1, source_target_pairs={{0,480},{4,484},{8,488},{12,492},{16,496},{20,500},{24,504},{28,50... | collective-permute-start | bytes 36872 | tf_op jit(solution)/shard_map/ppermute | solution.py:22
  179.0 87.2 %collective-permute-start.7 = (f32[8,384]{1,0:T(8,128)S(1)}, f32[8,384]{1,0:T(8,128)S(1)}, u32[]{:S(2)}, u32[]{:S(2)}) collective-permute-start(f32[8,384]{1,0:T(8,128)S(1)} %squeeze.98), channel_id=1, source_target_pairs={{0,32},{4,36},{8,40},{12,44},{16,48},{20,52},{24,56},{28,60},{32,6... | collective-permute-start | bytes 36872 | tf_op jit(solution)/shard_map/ppermute | solution.py:22
  (6 other events, 10.4 us)
